TPU v7x, 256 devices: a whole 4x4x8 slice. The times are simulated.
256 devices in a mesh: dp: 32 (over z, y), expert: 8 (over x, core).
Axes of the slice: x: 4, y: 4, z: 8, core: 2. Of those that a mesh axis runs over, the one named last changes fastest.
Arguments:
- tokens: bfloat16 [32768, 2048], P(('dp', 'expert')), may hold values from -6 to 6
- routes: int32 [32768, 2], P(('dp', 'expert')), may hold values from 0 to 127, all different within a row; in each aligned block of 128 rows (0 to 127, 128 to 255, ...) at most 4 rows name the same one
- gate_codes: int32 [32768, 2], P(('dp', 'expert')), may hold values from 1 to 1024
- w_gate: bfloat16 [256, 2048, 384], P(('dp', 'expert')), may hold values from -0.125 to 0.125
- w_up: bfloat16 [256, 2048, 384], P(('dp', 'expert')), may hold values from -0.125 to 0.125
- w_down: bfloat16 [256, 384, 2048], P(('dp', 'expert')), may hold values from -0.21875 to 0.21875
- cot: bfloat16 [32768, 2048], P(('dp', 'expert')), may hold values from -6 to 6
Outputs:
- mixed: bfloat16 [32768, 2048], P(('dp', 'expert'))
- d_tokens: bfloat16 [32768, 2048], P(('dp', 'expert'))
- d_gate: bfloat16 [256, 2048, 384], P(('dp', 'expert'))
- d_up: bfloat16 [256, 2048, 384], P(('dp', 'expert'))
- d_down: bfloat16 [256, 384, 2048], P(('dp', 'expert'))
Inputs may be any that keep to these rules, and one draw needn't show every extreme that they name: `routes`: each row names 2 different experts; among the 128 rows of one device no expert is named more than 4 times, a bound that some block reaches. `gate_codes`: the gate weight is the value divided by 1024.
All inputs are finite; a program needn't handle non-finite values.
Results may differ from a plain program's by a relative error of at most 0.012.
Values may be sent and summed in bfloat16 or wider, within the bound.
No kernel may reach another device: no remote copies, remote signals or barrier semaphores. Data moves between devices by JAX's collectives and lax.ppermute only.
A program may use at most 128 MiB of HBM per device.

v0:
```python
import jax
import jax.numpy as jnp
from jax import lax
from jax.sharding import PartitionSpec as P


def expert_work(xrows, qrows, w_gate, w_up, w_down):
    act = jnp.dot(xrows, w_gate, preferred_element_type=jnp.float32)
    upv = jnp.dot(xrows, w_up, preferred_element_type=jnp.float32)
    sig = jax.nn.sigmoid(act)
    silu = act * sig
    hidden = (silu * upv).astype(jnp.bfloat16)
    outv = jnp.dot(hidden, w_down, preferred_element_type=jnp.float32).astype(jnp.bfloat16)
    dhid = jnp.dot(qrows, w_down.T, preferred_element_type=jnp.float32)
    dact = (dhid * upv * sig * (1.0 + act * (1.0 - sig))).astype(jnp.bfloat16)
    dupv = (dhid * silu).astype(jnp.bfloat16)
    pgrad = (
        jnp.dot(dact, w_gate.T, preferred_element_type=jnp.float32)
        + jnp.dot(dupv, w_up.T, preferred_element_type=jnp.float32)
    ).astype(jnp.bfloat16)
    grad_g = jnp.dot(xrows.T, dact, preferred_element_type=jnp.float32).astype(jnp.bfloat16)
    grad_u = jnp.dot(xrows.T, dupv, preferred_element_type=jnp.float32).astype(jnp.bfloat16)
    grad_d = jnp.dot(hidden.T, qrows, preferred_element_type=jnp.float32).astype(jnp.bfloat16)
    return (outv, pgrad, grad_g, grad_u, grad_d)


def reorder(index, n_data, n_group, slots):
    device = index // slots
    within = index % slots
    return (device % n_group * n_data + device // n_group) * slots + within


def group_major(row_pair, n_data, n_group, slots):
    return row_pair.reshape(n_data, n_group, slots).transpose(1, 0, 2).reshape(-1)


def local(tokens, routes, gate_codes, w_gate, w_up, w_down, cot):
    tok_rows, top = routes.shape
    width = tokens.shape[1]
    n_data = lax.axis_size("dp")
    n_group = lax.axis_size("expert")
    devices = n_data * n_group
    experts = devices // 2
    most = max(2, 2 * tok_rows * top // experts)
    pairs = tok_rows * top
    expert_ids = routes.reshape(pairs)
    onehot = (expert_ids[:, None] == jnp.arange(experts, dtype=jnp.int32)[None, :]).astype(
        jnp.int32
    )
    before = jnp.cumsum(onehot, axis=0) - onehot
    position = jnp.sum(before * onehot, axis=1)
    gates = gate_codes.reshape(pairs).astype(jnp.float32) / 1024.0
    qpairs = (
        (gates.reshape(tok_rows, top, 1) * cot.astype(jnp.float32)[:, None, :])
        .astype(jnp.bfloat16)
        .reshape(pairs, width)
    )
    tok_pad = jnp.concatenate([tokens, jnp.zeros((1, width), jnp.bfloat16)], axis=0)
    q_pad = jnp.concatenate([qpairs, jnp.zeros((1, width), jnp.bfloat16)], axis=0)
    pair_ids = jnp.arange(pairs, dtype=jnp.int32)
    wg = w_gate[0]
    wu = w_up[0]
    wd = w_down[0]
    total = devices * most
    halves = jnp.arange(2, dtype=jnp.int32)
    targets = (2 * expert_ids[:, None] + halves[None, :]) * most + position[:, None]
    row_pair = (
        jnp.full((total,), pairs, jnp.int32).at[targets.reshape(-1)].set(jnp.repeat(pair_ids, 2))
    )
    row_pair = group_major(row_pair, n_data, n_group, most)
    row_token = jnp.where(row_pair < pairs, row_pair // top, tok_rows)
    xsend = tok_pad[row_token].reshape(n_group, n_data, most * width)
    qsend = q_pad[row_pair].reshape(n_group, n_data, most * width)
    xrecv, qrecv = (
        lax.all_to_all(
            lax.all_to_all(xsend, "dp", split_axis=1, concat_axis=1, tiled=True),
            "expert",
            split_axis=0,
            concat_axis=0,
            tiled=True,
        ),
        lax.all_to_all(
            lax.all_to_all(qsend, "dp", split_axis=1, concat_axis=1, tiled=True),
            "expert",
            split_axis=0,
            concat_axis=0,
            tiled=True,
        ),
    )
    outv, pgrad, grad_g, grad_u, grad_d = expert_work(
        xrecv.reshape(total, width), qrecv.reshape(total, width), wg, wu, wd
    )
    oback, pback = (
        lax.all_to_all(
            lax.all_to_all(
                outv.reshape(n_group, n_data, most * width),
                "dp",
                split_axis=1,
                concat_axis=1,
                tiled=True,
            ),
            "expert",
            split_axis=0,
            concat_axis=0,
            tiled=True,
        ),
        lax.all_to_all(
            lax.all_to_all(
                pgrad.reshape(n_group, n_data, most * width),
                "dp",
                split_axis=1,
                concat_axis=1,
                tiled=True,
            ),
            "expert",
            split_axis=0,
            concat_axis=0,
            tiled=True,
        ),
    )
    back_idx = reorder(targets, n_data, n_group, most)
    pair_out = jnp.sum(oback.reshape(total, width)[back_idx].astype(jnp.float32), axis=1)
    pair_grad = jnp.sum(pback.reshape(total, width)[back_idx].astype(jnp.float32), axis=1)
    mixed = jnp.sum((gates[:, None] * pair_out).reshape(tok_rows, top, width), axis=1).astype(
        jnp.bfloat16
    )
    d_tokens = jnp.sum(pair_grad.reshape(tok_rows, top, width), axis=1).astype(jnp.bfloat16)
    return (mixed, d_tokens, grad_g[None], grad_u[None], grad_d[None])


def solution(mesh):
    placed = (
        P(("dp", "expert"), None),
        P(("dp", "expert"), None),
        P(("dp", "expert"), None),
        P(("dp", "expert"), None, None),
        P(("dp", "expert"), None, None),
        P(("dp", "expert"), None, None),
        P(("dp", "expert"), None),
    )
    return jax.shard_map(
        local,
        mesh=mesh,
        in_specs=placed,
        out_specs=(
            P(("dp", "expert"), None),
            P(("dp", "expert"), None),
            P(("dp", "expert"), None, None),
            P(("dp", "expert"), None, None),
            P(("dp", "expert"), None, None),
        ),
        check_vma=False,
    )
```

profile of v0, /device:TPU:32, one launch (start us, length us, event | category | flops | bytes accessed | tf_op | source)
XLA Modules:
  0.0 741.6 jit_solution(10845163730356967747)
XLA Ops:
  11.9 7.9 %reshape.463 = bf16[8,32,8192]{2,1,0:T(8,128)(2,1)} reshape(bf16[1024,2048]{1,0:T(8,128)(2,1)} %gather_fusion) | data formatting | bytes 8388608 | tf_op jit(solution)/shard_map/reshape | solution.py:72
  26.2 11.5 %all-to-all-start = ((bf16[8,32,8192]{2,0,1:T(8,128)(2,1)}), bf16[8,32,8192]{2,0,1:T(8,128)(2,1)}, u32[]{:S(2)}, u32[]{:S(2)}) async-start(bf16[8,32,8192]{2,0,1:T(8,128)(2,1)} %copy.83), calls=%async_computation | async-start | bytes 8388608 | tf_op jit(solution)/shard_map/all_to_all | solution.py:76
  52.1 7.9 %reshape.467 = bf16[8,32,8192]{2,1,0:T(8,128)(2,1)} reshape(bf16[1024,2048]{1,0:T(8,128)(2,1)} %gather_fusion.2) | data formatting | bytes 8388608 | tf_op jit(solution)/shard_map/reshape | solution.py:73
  66.5 66.0 %all-to-all-done = bf16[8,32,8192]{2,0,1:T(8,128)(2,1)} async-done(((bf16[8,32,8192]{2,0,1:T(8,128)(2,1)}), bf16[8,32,8192]{2,0,1:T(8,128)(2,1)}, u32[]{:S(2)}, u32[]{:S(2)}) %all-to-all-start) | async-done | bytes 4194336 | tf_op jit(solution)/shard_map/all_to_all | solution.py:76
  132.5 18.0 %all-to-all-start.4 = ((bf16[8,32,8192]{2,0,1:T(8,128)(2,1)}), bf16[8,32,8192]{2,0,1:T(8,128)(2,1)}, u32[]{:S(2)}, u32[]{:S(2)}) async-start(bf16[8,32,8192]{2,0,1:T(8,128)(2,1)} %copy.89), calls=%async_computation.4 | async-start | bytes 8388608 | tf_op jit(solution)/shard_map/all_to_all | solution.py:83
  156.9 88.2 %all-to-all-done.4 = bf16[8,32,8192]{2,0,1:T(8,128)(2,1)} async-done(((bf16[8,32,8192]{2,0,1:T(8,128)(2,1)}), bf16[8,32,8192]{2,0,1:T(8,128)(2,1)}, u32[]{:S(2)}, u32[]{:S(2)}) %all-to-all-start.4) | async-done | bytes 4194336 | tf_op jit(solution)/shard_map/all_to_all | solution.py:83
  256.1 43.2 %all-to-all-done.1 = bf16[8,32,8192]{2,1,0:T(8,128)(2,1)} async-done(((bf16[8,32,8192]{2,1,0:T(8,128)(2,1)}), bf16[8,32,8192]{2,1,0:T(8,128)(2,1)}, u32[]{:S(2)}, u32[]{:S(2)}) %all-to-all-start.1) | async-done | bytes 4194336 | tf_op jit(solution)/shard_map/all_to_all | solution.py:75
  304.0 7.9 %reshape.464 = bf16[1024,2048]{1,0:T(8,128)(2,1)} reshape(bf16[8,32,8192]{2,1,0:T(8,128)(2,1)} %all-to-all-done.1) | data formatting | bytes 8388608 | tf_op jit(solution)/shard_map/reshape | solution.py:91
  321.6 32.0 %all-to-all-done.5 = bf16[8,32,8192]{2,1,0:T(8,128)(2,1)} async-done(((bf16[8,32,8192]{2,1,0:T(8,128)(2,1)}), bf16[8,32,8192]{2,1,0:T(8,128)(2,1)}, u32[]{:S(2)}, u32[]{:S(2)}) %all-to-all-start.5) | async-done | bytes 4194336 | tf_op jit(solution)/shard_map/all_to_all | solution.py:82
  353.6 8.0 %reshape.468 = bf16[1024,2048]{1,0:T(8,128)(2,1)} reshape(bf16[8,32,8192]{2,1,0:T(8,128)(2,1)} %all-to-all-done.5) | data formatting | bytes 8388608 | tf_op jit(solution)/shard_map/reshape | solution.py:91
  361.6 7.1 multiply_convert_fusion.1
  373.9 7.9 %reshape.465 = bf16[8,32,8192]{2,1,0:T(8,128)(2,1)} reshape(bf16[1024,2048]{1,0:T(8,128)(2,1)} %convolution_convert_fusion) | data formatting | bytes 8388608 | tf_op jit(solution)/shard_map/reshape | solution.py:96
  388.2 7.4 all-to-all-start.2
  403.6 7.9 %reshape.469 = bf16[8,32,8192]{2,1,0:T(8,128)(2,1)} reshape(bf16[1024,2048]{1,0:T(8,128)(2,1)} %add_convert_fusion) | data formatting | bytes 8388608 | tf_op jit(solution)/shard_map/reshape | solution.py:109
  418.0 71.8 %all-to-all-done.2 = bf16[8,32,8192]{2,0,1:T(8,128)(2,1)} async-done(((bf16[8,32,8192]{2,0,1:T(8,128)(2,1)}), bf16[8,32,8192]{2,0,1:T(8,128)(2,1)}, u32[]{:S(2)}, u32[]{:S(2)}) %all-to-all-start.2) | async-done | bytes 4194336 | tf_op jit(solution)/shard_map/all_to_all | solution.py:95
  489.8 6.7 all-to-all-start.6
  502.9 88.4 %all-to-all-done.6 = bf16[8,32,8192]{2,0,1:T(8,128)(2,1)} async-done(((bf16[8,32,8192]{2,0,1:T(8,128)(2,1)}), bf16[8,32,8192]{2,0,1:T(8,128)(2,1)}, u32[]{:S(2)}, u32[]{:S(2)}) %all-to-all-start.6) | async-done | bytes 4194336 | tf_op jit(solution)/shard_map/all_to_all | solution.py:108
  602.4 43.2 %all-to-all-done.3 = bf16[8,32,8192]{2,1,0:T(8,128)(2,1)} async-done(((bf16[8,32,8192]{2,1,0:T(8,128)(2,1)}), bf16[8,32,8192]{2,1,0:T(8,128)(2,1)}, u32[]{:S(2)}, u32[]{:S(2)}) %all-to-all-start.3) | async-done | bytes 4194336 | tf_op jit(solution)/shard_map/all_to_all | solution.py:94
  663.4 7.9 %reshape.466 = bf16[1024,2048]{1,0:T(8,128)(2,1)} reshape(bf16[8,32,8192]{2,1,0:T(8,128)(2,1)} %all-to-all-done.3) | data formatting | bytes 8388608 | tf_op jit(solution)/shard_map/reshape | solution.py:122
  671.2 8.0 %gather_fusion.1 = bf16[512,2048]{1,0:T(8,128)(2,1)} fusion(bf16[1024,2048]{1,0:T(8,128)(2,1)} %reshape.466, s32[1024]{0:T(1024)S(1)} %pad_clamp_fusion), kind=kCustom, calls=%fused_computation.1 | custom fusion | bytes 4196352 | tf_op jit(solution)/shard_map/gather | solution.py:122
  684.9 8.5 %reduce_sum.48 = f32[256,2048]{1,0:T(8,128)} reduce(f32[256,2,2048]{2,1,0:T(2,128)} %reshape.514, f32[]{:T(128)} %constant.88.clone.1), dimensions={1}, to_apply=%region_4.5 | reduce | flops 524288 | bytes 6291460 | tf_op jit(solution)/shard_map/reduce_sum | solution.py:122
  702.5 7.9 %reshape.470 = bf16[1024,2048]{1,0:T(8,128)(2,1)} reshape(bf16[8,32,8192]{2,1,0:T(8,128)(2,1)} %all-to-all-done.7) | data formatting | bytes 8388608 | tf_op jit(solution)/shard_map/reshape | solution.py:123
  710.4 8.2 %gather_fusion.3 = bf16[512,2048]{1,0:T(8,128)(2,1)} fusion(bf16[1024,2048]{1,0:T(8,128)(2,1)} %reshape.470, s32[1024]{0:T(1024)S(1)} %pad_clamp_fusion), kind=kCustom, calls=%fused_computation.3 | custom fusion | bytes 4196352 | tf_op jit(solution)/shard_map/gather | solution.py:123
  724.1 8.5 %reduce_sum.51 = f32[256,2048]{1,0:T(8,128)} reduce(f32[256,2,2048]{2,1,0:T(2,128)} %reshape.515, f32[]{:T(128)} %constant.88.clone.1), dimensions={1}, to_apply=%region_6.7 | reduce | flops 524288 | bytes 6291460 | tf_op jit(solution)/shard_map/reduce_sum | solution.py:123
  (93 shorter events, 160.0 us)
Async XLA Ops:
  0.6 361.0 %copy-start = (bf16[1,384,2048]{2,1,0:T(8,128)(2,1)S(1)}, bf16[1,384,2048]{2,1,0:T(8,128)(2,1)}, u32[]{:S(2)}) copy-start(bf16[1,384,2048]{2,1,0:T(8,128)(2,1)} %param.12) | copy-start | bytes 4718596
  0.6 5.1 copy-start.10
  26.2 11.6 %copy-start.11 = (s32[128,2]{0,1:T(2,128)S(1)}, s32[128,2]{0,1:T(2,128)}, u32[]{:S(2)}) copy-start(s32[128,2]{0,1:T(2,128)} %param.9) | copy-start | bytes 3076
  26.2 11.8 %copy-start.9 = (bf16[128,2048]{1,0:T(8,128)(2,1)S(1)}, bf16[128,2048]{1,0:T(8,128)(2,1)}, u32[]{:S(2)}) copy-start(bf16[128,2048]{1,0:T(8,128)(2,1)} %param.13) | copy-start | bytes 1572868
  26.2 106.2 %all-to-all-start = ((bf16[8,32,8192]{2,0,1:T(8,128)(2,1)}), bf16[8,32,8192]{2,0,1:T(8,128)(2,1)}, u32[]{:S(2)}, u32[]{:S(2)}) async-start(bf16[8,32,8192]{2,0,1:T(8,128)(2,1)} %copy.83), calls=%async_computation | async-start | bytes 8388608 | tf_op jit(solution)/shard_map/all_to_all | solution.py:76
  132.5 112.6 %all-to-all-start.4 = ((bf16[8,32,8192]{2,0,1:T(8,128)(2,1)}), bf16[8,32,8192]{2,0,1:T(8,128)(2,1)}, u32[]{:S(2)}, u32[]{:S(2)}) async-start(bf16[8,32,8192]{2,0,1:T(8,128)(2,1)} %copy.89), calls=%async_computation.4 | async-start | bytes 8388608 | tf_op jit(solution)/shard_map/all_to_all | solution.py:83
  245.1 54.2 %all-to-all-start.1 = ((bf16[8,32,8192]{2,1,0:T(8,128)(2,1)}), bf16[8,32,8192]{2,1,0:T(8,128)(2,1)}, u32[]{:S(2)}, u32[]{:S(2)}) async-start(bf16[8,32,8192]{2,1,0:T(8,128)(2,1)} %copy.84), calls=%async_computation.1 | async-start | bytes 8388608 | tf_op jit(solution)/shard_map/all_to_all | solution.py:75
  299.4 54.3 %all-to-all-start.5 = ((bf16[8,32,8192]{2,1,0:T(8,128)(2,1)}), bf16[8,32,8192]{2,1,0:T(8,128)(2,1)}, u32[]{:S(2)}, u32[]{:S(2)}) async-start(bf16[8,32,8192]{2,1,0:T(8,128)(2,1)} %copy.90), calls=%async_computation.5 | async-start | bytes 8388608 | tf_op jit(solution)/shard_map/all_to_all | solution.py:82
  311.9 6.3 copy-start.2
  311.9 6.3 copy-start.4
  368.7 0.9 copy-start.12
  388.2 101.6 %all-to-all-start.2 = ((bf16[8,32,8192]{2,0,1:T(8,128)(2,1)}), bf16[8,32,8192]{2,0,1:T(8,128)(2,1)}, u32[]{:S(2)}, u32[]{:S(2)}) async-start(bf16[8,32,8192]{2,0,1:T(8,128)(2,1)} %copy.85), calls=%async_computation.2 | async-start | bytes 8388608 | tf_op jit(solution)/shard_map/all_to_all | solution.py:95
  395.6 3.7 copy-start.5
  395.6 3.7 copy-start.7
  489.8 101.5 %all-to-all-start.6 = ((bf16[8,32,8192]{2,0,1:T(8,128)(2,1)}), bf16[8,32,8192]{2,0,1:T(8,128)(2,1)}, u32[]{:S(2)}, u32[]{:S(2)}) async-start(bf16[8,32,8192]{2,0,1:T(8,128)(2,1)} %copy.91), calls=%async_computation.6 | async-start | bytes 8388608 | tf_op jit(solution)/shard_map/all_to_all | solution.py:108
  591.3 54.2 %all-to-all-start.3 = ((bf16[8,32,8192]{2,1,0:T(8,128)(2,1)}), bf16[8,32,8192]{2,1,0:T(8,128)(2,1)}, u32[]{:S(2)}, u32[]{:S(2)}) async-start(bf16[8,32,8192]{2,1,0:T(8,128)(2,1)} %copy.86), calls=%async_computation.3 | async-start | bytes 8388608 | tf_op jit(solution)/shard_map/all_to_all | solution.py:94
  602.4 48.5 %copy-start.13 = (bf16[1024,384]{1,0:T(8,128)(2,1)S(1)}, bf16[1024,384]{1,0:T(8,128)(2,1)}, u32[]{:S(2)}) copy-start(bf16[1024,384]{1,0:T(8,128)(2,1)} %copy-done.12) | copy-start | bytes 2359300
  645.6 56.9 %all-to-all-start.7 = ((bf16[8,32,8192]{2,1,0:T(8,128)(2,1)}), bf16[8,32,8192]{2,1,0:T(8,128)(2,1)}, u32[]{:S(2)}, u32[]{:S(2)}) async-start(bf16[8,32,8192]{2,1,0:T(8,128)(2,1)} %copy.92), calls=%async_computation.7 | async-start | bytes 8388608 | tf_op jit(solution)/shard_map/all_to_all | solution.py:107
  650.8 5.4 copy-start.3
  650.8 5.3 copy-start.8
  656.2 3.6 copy-start.6
  732.6 8.6 %copy-start.1 = (bf16[1,384,2048]{2,1,0:T(8,128)(2,1)S(1)}, bf16[1,384,2048]{2,1,0:T(8,128)(2,1)}, u32[]{:S(2)}) copy-start(bf16[1,384,2048]{2,1,0:T(8,128)(2,1)} %param.12) | copy-start | bytes 4718596
where the time goes:
time: 756 us; the launch traced here: 742 us
  waiting for transfers between devices  433 us (57%)
  local copies, waits for them, and re-layouts  173 us (23%)
  starting transfers between devices  62 us (8%)
  matrix products  41.6 us (6%)
  other arithmetic  30.3 us (4%)
    all_to_all x1, waiting for transfers between devices, local(): lax.all_to_all(pgrad.reshape(n_group, n_data, most * width), 'dp', split_...  88.4 us
    all_to_all x1, waiting for transfers between devices, local(): lax.all_to_all(qsend, 'dp', split_axis=1, concat_axis=1, tiled=True)  88.2 us
    all_to_all x1, waiting for transfers between devices, local(): lax.all_to_all(outv.reshape(n_group, n_data, most * width), 'dp', split_a...  71.8 us
    all_to_all x1, waiting for transfers between devices, local(): lax.all_to_all(xsend, 'dp', split_axis=1, concat_axis=1, tiled=True)  66 us
    all_to_all x1, waiting for transfers between devices, local(): lax.all_to_all(lax.all_to_all(xsend, 'dp', split_axis=1, concat_axis=1, t...  43.2 us
    all_to_all x1, waiting for transfers between devices, local(): lax.all_to_all(lax.all_to_all(outv.reshape(n_group, n_data, most * width)...  43.2 us
    all_to_all x1, waiting for transfers between devices, local(): lax.all_to_all(lax.all_to_all(qsend, 'dp', split_axis=1, concat_axis=1, t...  32 us
    all_to_all x1, starting transfers between devices, local(): lax.all_to_all(qsend, 'dp', split_axis=1, concat_axis=1, tiled=True)  18 us
  transfers between devices with their start and end apart: 8, of which 7 were waited for; matrix products, arithmetic and copies ran while one was open for 20% of the time, Pallas kernels for 0%

commit v1 on v0

v1 whole, which is shorter than its diff:
```python
import jax
import jax.numpy as jnp
from jax import lax
from jax.sharding import Mesh
from jax.sharding import PartitionSpec as P

CHIPS = ("dp", "x")


def expert_work(xrows, qrows, wg, wu, wd):
    act = jnp.dot(xrows, wg, preferred_element_type=jnp.float32)
    upv = jnp.dot(xrows, wu, preferred_element_type=jnp.float32)
    sig = jax.nn.sigmoid(act)
    silu = act * sig
    hidden = (silu * upv).astype(jnp.bfloat16)
    outv = jnp.dot(hidden, wd, preferred_element_type=jnp.float32).astype(jnp.bfloat16)
    dhid = jnp.dot(qrows, wd.T, preferred_element_type=jnp.float32)
    dact = (dhid * upv * sig * (1.0 + act * (1.0 - sig))).astype(jnp.bfloat16)
    dupv = (dhid * silu).astype(jnp.bfloat16)
    pgrad = (
        jnp.dot(dact, wg.T, preferred_element_type=jnp.float32)
        + jnp.dot(dupv, wu.T, preferred_element_type=jnp.float32)
    ).astype(jnp.bfloat16)
    grad_g = jnp.dot(xrows.T, dact, preferred_element_type=jnp.float32)
    grad_u = jnp.dot(xrows.T, dupv, preferred_element_type=jnp.float32)
    grad_d = jnp.dot(hidden.T, qrows, preferred_element_type=jnp.float32)
    return outv, pgrad, grad_g, grad_u, grad_d


def local(tokens, routes, gate_codes, w_gate, w_up, w_down, cot):
    tok_rows, top = routes.shape
    width = tokens.shape[1]
    half = w_gate.shape[2]
    chips = lax.axis_size("dp") * lax.axis_size("x")
    pairs = tok_rows * top
    most = max(1, 2 * pairs // chips)
    slots = chips * most
    core = lax.axis_index("core")
    swap = [(0, 1), (1, 0)]

    wg_o, wu_o, wd_o = lax.ppermute((w_gate[0], w_up[0], w_down[0]), "core", swap)
    first = core == 0
    wg = jnp.where(first, jnp.concatenate([w_gate[0], wg_o], 1), jnp.concatenate([wg_o, w_gate[0]], 1))
    wu = jnp.where(first, jnp.concatenate([w_up[0], wu_o], 1), jnp.concatenate([wu_o, w_up[0]], 1))
    wd = jnp.where(first, jnp.concatenate([w_down[0], wd_o], 0), jnp.concatenate([wd_o, w_down[0]], 0))

    expert_ids = routes.reshape(pairs)
    onehot = (expert_ids[:, None] == jnp.arange(chips, dtype=jnp.int32)[None, :]).astype(jnp.int32)
    before = jnp.cumsum(onehot, axis=0) - onehot
    position = jnp.sum(before * onehot, axis=1)
    slot = expert_ids * most + position
    gates = gate_codes.reshape(pairs).astype(jnp.float32) / 1024.0
    qpairs = (
        (gates.reshape(tok_rows, top, 1) * cot.astype(jnp.float32)[:, None, :])
        .astype(jnp.bfloat16)
        .reshape(pairs, width)
    )
    pick = (slot.reshape(tok_rows, top).T[:, :, None] == jnp.arange(slots, dtype=jnp.int32)[None, None, :])
    pick = pick.astype(jnp.bfloat16)
    sel_x = pick[0] + pick[1]
    xs = jnp.dot(sel_x.T, tokens, preferred_element_type=jnp.float32).astype(jnp.bfloat16)
    sel_q = pick.transpose(2, 1, 0).reshape(slots, pairs)
    qs = jnp.dot(sel_q, qpairs, preferred_element_type=jnp.float32).astype(jnp.bfloat16)
    send = jnp.concatenate([xs, qs], axis=1).reshape(chips, most, 2 * width)
    recv = lax.all_to_all(send, CHIPS, 0, 0, tiled=True).reshape(slots, 2 * width)

    outv, pgrad, grad_g, grad_u, grad_d = expert_work(recv[:, :width], recv[:, width:], wg, wu, wd)

    back = jnp.concatenate([outv, pgrad], axis=1).reshape(chips, most, 2 * width)
    got = lax.all_to_all(back, CHIPS, 0, 0, tiled=True).reshape(slots, 2 * width)

    g_lo, g_hi = grad_g[:, :half], grad_g[:, half:]
    u_lo, u_hi = grad_u[:, :half], grad_u[:, half:]
    d_lo, d_hi = grad_d[:half], grad_d[half:]
    mine = (jnp.where(first, g_lo, g_hi), jnp.where(first, u_lo, u_hi), jnp.where(first, d_lo, d_hi))
    other = (jnp.where(first, g_hi, g_lo), jnp.where(first, u_hi, u_lo), jnp.where(first, d_hi, d_lo))
    came = lax.ppermute(other, "core", swap)
    d_gate = (mine[0] + came[0]).astype(jnp.bfloat16)
    d_up = (mine[1] + came[1]).astype(jnp.bfloat16)
    d_down = (mine[2] + came[2]).astype(jnp.bfloat16)

    o_k = jnp.einsum("kts,sw->ktw", pick, got[:, :width], preferred_element_type=jnp.float32)
    mixed = (gates.reshape(tok_rows, top).T[:, :, None] * o_k).sum(0).astype(jnp.bfloat16)
    d_tokens = jnp.dot(sel_x, got[:, width:], preferred_element_type=jnp.float32).astype(jnp.bfloat16)
    return (mixed, d_tokens, d_gate[None], d_up[None], d_down[None])


def solution(mesh):
    n_data = mesh.shape["dp"]
    n_group = mesh.shape["expert"]
    fine = Mesh(mesh.devices.reshape(n_data, n_group // 2, 2), ("dp", "x", "core"))
    rows = P(("dp", "x", "core"), None)
    stack = P(("dp", "x", "core"), None, None)
    return jax.shard_map(
        local,
        mesh=fine,
        in_specs=(rows, rows, rows, stack, stack, stack, rows),
        out_specs=(rows, rows, stack, stack, stack),
        check_vma=False,
    )
```

time: 756 us -> 289 us (0.38); the launches traced: 742 us -> 288 us
  waiting for transfers between devices: 433 us -> 171 us
  local copies, waits for them, and re-layouts: 173 us -> 31.7 us
  starting transfers between devices: 62 us -> 25.9 us
  other arithmetic: 30.3 us -> 17.5 us
    all_to_all x8 -> x2, waiting for transfers between devices: 433 us -> 169 us  [the longest x1 95.1 us: local(): lax.all_to_all(send, CHIPS, 0, 0, tiled=True).reshape(slots, 2 * width)]
    reshape x16 -> x4, local copies, waits for them, and re-layouts: 93 us -> 28.2 us  [the longest x1 7.19 us: local(): send = jnp.concatenate([xs, qs], axis=1).reshape(chips, most, 2 * width)]
    all_to_all x8 -> x2, starting transfers between devices: 62 us -> 24.6 us  [the longest x1 15.6 us: local(): lax.all_to_all(send, CHIPS, 0, 0, tiled=True).reshape(slots, 2 * width)]
    gather x4 -> x0, local copies, waits for them, and re-layouts: 28.3 us -> none  [the longest x1 8.23 us: local(): pback.reshape(total, width)[back_idx].astype(jnp.float32)]
    reduce_sum x4 -> x0, other arithmetic: 27.6 us -> none  [the longest x1 8.53 us: local(): jnp.sum(oback.reshape(total, width)[back_idx].astype(jnp.float32), axis=1)]
    all_to_all x4 -> x0, local copies, waits for them, and re-layouts: 25.8 us -> none  [the longest x1 6.46 us: local(): lax.all_to_all(outv.reshape(n_group, n_data, most * width), 'dp', split_a...]
    convert_element_type x2 -> x0, local copies, waits for them, and re-layouts: 11.1 us -> none  [the longest x1 5.64 us: local(): oback.reshape(total, width)[back_idx].astype(jnp.float32)]
    dot_general x9 -> x13, matrix products: 41.6 us -> 40.4 us  [the longest x1 5.62 us: expert_work(): act = jnp.dot(xrows, wg, preferred_element_type=jnp.float32)]
  transfers between devices with their start and end apart: 8 -> 8, of which waited for: 7 -> 3; matrix products, arithmetic and copies ran while one was open for 20% -> 11% of each run, Pallas kernels for 0% -> 0%
where the time goes in v1:
time: 289 us; the launch traced here: 288 us
  waiting for transfers between devices  171 us (59%)
  matrix products  40.4 us (14%)
  local copies, waits for them, and re-layouts  31.7 us (11%)
  starting transfers between devices  25.9 us (9%)
  other arithmetic  17.5 us (6%)
    all_to_all x1, waiting for transfers between devices, local(): lax.all_to_all(send, CHIPS, 0, 0, tiled=True).reshape(slots, 2 * width)  95.1 us
    all_to_all x1, waiting for transfers between devices, local(): lax.all_to_all(back, CHIPS, 0, 0, tiled=True).reshape(slots, 2 * width)  73.5 us
    all_to_all x1, starting transfers between devices, local(): lax.all_to_all(send, CHIPS, 0, 0, tiled=True).reshape(slots, 2 * width)  15.6 us
    all_to_all x1, starting transfers between devices, local(): lax.all_to_all(back, CHIPS, 0, 0, tiled=True).reshape(slots, 2 * width)  9 us
    reshape x1, local copies, waits for them, and re-layouts, local(): send = jnp.concatenate([xs, qs], axis=1).reshape(chips, most, 2 * width)  7.19 us
    reshape x1, local copies, waits for them, and re-layouts, local(): jnp.concatenate([outv, pgrad], axis=1).reshape(chips, most, 2 * width)  7.17 us
    reshape x1, local copies, waits for them, and re-layouts, local(): lax.all_to_all(back, CHIPS, 0, 0, tiled=True).reshape(slots, 2 * width)  6.96 us
    reshape x1, local copies, waits for them, and re-layouts, local(): lax.all_to_all(send, CHIPS, 0, 0, tiled=True).reshape(slots, 2 * width)  6.91 us
  transfers between devices with their start and end apart: 8, of which 3 were waited for; matrix products, arithmetic and copies ran while one was open for 11% of the time, Pallas kernels for 0%

profile of v1, /device:TPU:32, one launch (start us, length us, event | category | flops | bytes accessed | tf_op | source)
XLA Modules:
  0.0 287.8 jit_solution(524545170610779265)
XLA Ops:
  6.8 2.5 pad_maximum_fusion
  9.3 7.2 %reshape.56 = bf16[128,4,4096]{2,1,0:T(4,128)(2,1)} reshape(bf16[512,4096]{1,0:T(8,128)(2,1)} %pad_maximum_fusion) | data formatting | bytes 8388608 | tf_op jit(solution)/shard_map/reshape | solution.py:64
  16.5 15.6 %all-to-all-start = ((bf16[128,4,4096]{2,1,0:T(4,128)(2,1)}), bf16[128,4,4096]{2,1,0:T(4,128)(2,1)}, u32[]{:S(2)}, u32[]{:S(2)}) async-start(bf16[128,4,4096]{2,1,0:T(4,128)(2,1)} %reshape.56), calls=%async_computation | async-start | bytes 8388608 | tf_op jit(solution)/shard_map/all_to_all | solution.py:65
  32.8 95.1 %all-to-all-done = bf16[128,4,4096]{2,1,0:T(4,128)(2,1)} async-done(((bf16[128,4,4096]{2,1,0:T(4,128)(2,1)}), bf16[128,4,4096]{2,1,0:T(4,128)(2,1)}, u32[]{:S(2)}, u32[]{:S(2)}) %all-to-all-start) | async-done | bytes 4194336 | tf_op jit(solution)/shard_map/all_to_all | solution.py:65
  127.9 6.9 %reshape.57 = bf16[512,4096]{1,0:T(8,128)(2,1)} reshape(bf16[128,4,4096]{2,1,0:T(4,128)(2,1)} %all-to-all-done) | data formatting | bytes 8388608 | tf_op jit(solution)/shard_map/reshape | solution.py:65
  134.8 5.6 %fusion.16 = f32[512,768]{1,0:T(8,128)S(1)} fusion(bf16[512,4096]{1,0:T(8,128)(2,1)} %reshape.57, bf16[2048,384]{1,0:T(8,128)(2,1)} %collective-permute-done, bf16[2048,384]{1,0:T(8,128)(2,1)} %bitcast.55, pred[]{:T(512)S(6)} %eq.62), kind=kOutput, calls=%fused_computation.39 | convolution fusion | flops 1624768512 | bytes 6815745 | tf_op jit(solution)/shard_map/dot_general | solution.py:11
  140.5 3.7 %fusion.3 = f32[512,768]{1,0:T(8,128)S(1)} fusion(bf16[512,4096]{1,0:T(8,128)(2,1)S(1)} %copy-done.2, bf16[384,2048]{1,0:T(8,128)(2,1)} %collective-permute-done.2, bf16[384,2048]{1,0:T(8,128)(2,1)S(1)} %bitcast.52, pred[]{:T(512)S(6)} %eq.62), kind=kOutput, calls=%fused_computation.22 | convolution fusion | flops 1624768512 | bytes 6815745 | tf_op jit(solution)/shard_map/dot_general | solution.py:17
  144.3 4.4 %multiply_convert_fusion.3 = (bf16[512,768]{1,0:T(8,128)(2,1)S(1)}, bf16[512,768]{1,0:T(8,128)(2,1)S(1)}, bf16[512,768]{1,0:T(8,128)(2,1)S(1)}) fusion(f32[512,768]{1,0:T(8,128)S(1)} %fusion.16, f32[512,768]{1,0:T(8,128)S(1)} %fusion.3, bf16[2048,384]{1,0:T(8,128)(2,1)} %collective-permute-done.1, bf16[2048,384]{1,0:T(8,128)(2,1)S(1)} %bitcast.49, ...), kind=kOutput, calls=%fused_computation.29 | convolution fusion | flops 1630666752 | bytes 10747905 | tf_op jit(solution)/shard_map/dot_general | solution.py:12
  148.7 4.1 %fusion.20 = f32[512,2048]{1,0:T(8,128)S(1)} fusion(bf16[512,768]{1,0:T(8,128)(2,1)S(1)} %get-tuple-element.7, bf16[2048,384]{1,0:T(8,128)(2,1)} %collective-permute-done.1, bf16[2048,384]{1,0:T(8,128)(2,1)S(1)} %bitcast.50, pred[]{:T(512)S(6)} %eq.62), kind=kOutput, calls=%fused_computation.43 | convolution fusion | flops 1624768512 | bytes 8126465 | tf_op jit(solution)/shard_map/dot_general | solution.py:22
  152.8 3.8 %convolution_convert_fusion.1 = bf16[512,2048]{1,0:T(8,128)(2,1)S(1)} fusion(bf16[512,768]{1,0:T(8,128)(2,1)S(1)} %get-tuple-element.5, bf16[384,2048]{1,0:T(8,128)(2,1)} %collective-permute-done.2, bf16[384,2048]{1,0:T(8,128)(2,1)S(1)} %bitcast.53, pred[]{:T(512)S(6)} %eq.62), kind=kOutput, calls=%fused_computation.11 | convolution fusion | flops 1625817088 | bytes 6029313 | tf_op jit(solution)/shard_map/dot_general | solution.py:16
  156.7 3.9 %add_convert_fusion = bf16[512,2048]{1,0:T(8,128)(2,1)S(1)} fusion(f32[512,2048]{1,0:T(8,128)S(1)} %fusion.20, bf16[512,768]{1,0:T(8,128)(2,1)S(1)} %get-tuple-element.6, bf16[2048,384]{1,0:T(8,128)(2,1)} %collective-permute-done, bf16[2048,384]{1,0:T(8,128)(2,1)S(1)} %bitcast.56, pred[]{:T(512)S(6)} %eq.62), kind=kOutput, calls=%fused_computation.3 | convolution fusion | flops 1626865664 | bytes 10223617 | tf_op jit(solution)/shard_map/dot_general | solution.py:21
  160.6 2.5 pad_maximum_fusion.1
  163.0 7.2 %reshape.58 = bf16[128,4,4096]{2,1,0:T(4,128)(2,1)} reshape(bf16[512,4096]{1,0:T(8,128)(2,1)} %pad_maximum_fusion.1) | data formatting | bytes 8388608 | tf_op jit(solution)/shard_map/reshape | solution.py:69
  170.2 9.0 %all-to-all-start.1 = ((bf16[128,4,4096]{2,1,0:T(4,128)(2,1)}), bf16[128,4,4096]{2,1,0:T(4,128)(2,1)}, u32[]{:S(2)}, u32[]{:S(2)}) async-start(bf16[128,4,4096]{2,1,0:T(4,128)(2,1)} %reshape.58), calls=%async_computation.1 | async-start | bytes 8388608 | tf_op jit(solution)/shard_map/all_to_all | solution.py:70
  179.2 3.5 %fusion.12 = f32[2048,768]{1,0:T(8,128)S(1)} fusion(bf16[512,768]{1,0:T(8,128)(2,1)S(1)} %get-tuple-element.6, bf16[512,4096]{1,0:T(8,128)(2,1)} %reshape.57), kind=kOutput, calls=%fused_computation.35 | convolution fusion | flops 1610612736 | bytes 9175040 | tf_op jit(solution)/shard_map/dot_general | solution.py:24
  185.1 1.9 fusion.10
  187.0 1.9 slice_select_fusion.1
  190.8 2.1 slice_select_fusion
  196.6 2.6 collective-permute-done.5
  199.3 1.9 fusion.7
  201.2 73.5 %all-to-all-done.1 = bf16[128,4,4096]{2,1,0:T(4,128)(2,1)} async-done(((bf16[128,4,4096]{2,1,0:T(4,128)(2,1)}), bf16[128,4,4096]{2,1,0:T(4,128)(2,1)}, u32[]{:S(2)}, u32[]{:S(2)}) %all-to-all-start.1) | async-done | bytes 4194336 | tf_op jit(solution)/shard_map/all_to_all | solution.py:70
  274.7 7.0 %reshape.59 = bf16[512,4096]{1,0:T(8,128)(2,1)} reshape(bf16[128,4,4096]{2,1,0:T(4,128)(2,1)} %all-to-all-done.1) | data formatting | bytes 8388608 | tf_op jit(solution)/shard_map/reshape | solution.py:70
  281.6 2.8 convolution_convert_fusion.2
  284.5 3.3 %fusion.9 = bf16[128,2048]{1,0:T(8,128)(2,1)} fusion(bf16[512,4096]{1,0:T(8,128)(2,1)} %reshape.59, f32[2,128]{1,0:T(2,128)S(1)} %get-tuple-element.8, s32[2,128]{1,0:T(2,128)S(1)} %bitcast.47), kind=kOutput, calls=%fused_computation.32 | convolution fusion | flops 537788416 | bytes 2623488 | tf_op jit(solution)/shard_map/kts,sw->ktw/dot_general | solution.py:82
  (61 shorter events, 14.8 us)
Async XLA Ops:
  0.6 5.4 %copy-start = (bf16[128,2048]{1,0:T(8,128)(2,1)S(1)}, bf16[128,2048]{1,0:T(8,128)(2,1)}, u32[]{:S(2)}) copy-start(bf16[128,2048]{1,0:T(8,128)(2,1)} %param.7) | copy-start | bytes 1572868
  5.2 0.8 copy-start.8
  16.5 16.2 %copy-start.10 = (bf16[1,2048,384]{2,1,0:T(8,128)(2,1)S(1)}, bf16[1,2048,384]{2,1,0:T(8,128)(2,1)}, u32[]{:S(2)}) copy-start(bf16[1,2048,384]{2,1,0:T(8,128)(2,1)} %param.11) | copy-start | bytes 4718596
  16.5 111.4 %all-to-all-start = ((bf16[128,4,4096]{2,1,0:T(4,128)(2,1)}), bf16[128,4,4096]{2,1,0:T(4,128)(2,1)}, u32[]{:S(2)}, u32[]{:S(2)}) async-start(bf16[128,4,4096]{2,1,0:T(4,128)(2,1)} %reshape.56), calls=%async_computation | async-start | bytes 8388608 | tf_op jit(solution)/shard_map/all_to_all | solution.py:65
  32.1 102.7 %collective-permute-start = (bf16[2048,384]{1,0:T(8,128)(2,1)}, bf16[2048,384]{1,0:T(8,128)(2,1)}, u32[]{:S(2)}, u32[]{:S(2)}) collective-permute-start(bf16[2048,384]{1,0:T(8,128)(2,1)} %bitcast.54), channel_id=1, source_target_pairs={{0,1},{1,0},{2,3},{3,2},{4,5},{5,4},{6,7},{7,6},{8,9},{9,8},{10,11... | collective-permute-start | bytes 4718600 | tf_op jit(solution)/shard_map/ppermute | solution.py:41
  32.2 108.3 %collective-permute-start.2 = (bf16[384,2048]{1,0:T(8,128)(2,1)}, bf16[384,2048]{1,0:T(8,128)(2,1)}, u32[]{:S(2)}, u32[]{:S(2)}) collective-permute-start(bf16[384,2048]{1,0:T(8,128)(2,1)} %bitcast.51), channel_id=1, source_target_pairs={{0,1},{1,0},{2,3},{3,2},{4,5},{5,4},{6,7},{7,6},{8,9},{9,8},{10,11... | collective-permute-start | bytes 4718600 | tf_op jit(solution)/shard_map/ppermute | solution.py:41
  32.7 111.5 %collective-permute-start.1 = (bf16[2048,384]{1,0:T(8,128)(2,1)S(1)}, bf16[2048,384]{1,0:T(8,128)(2,1)}, u32[]{:S(2)}, u32[]{:S(2)}) collective-permute-start(bf16[2048,384]{1,0:T(8,128)(2,1)S(1)} %bitcast.48), channel_id=1, source_target_pairs={{0,1},{1,0},{2,3},{3,2},{4,5},{5,4},{6,7},{7,6},{8,9},{9,8},{10,11... | collective-permute-start | bytes 4718600 | tf_op jit(solution)/shard_map/ppermute | solution.py:41
  134.8 5.7 %copy-start.2 = (bf16[512,4096]{1,0:T(8,128)(2,1)S(1)}, bf16[512,4096]{1,0:T(8,128)(2,1)}, u32[]{:S(2)}) copy-start(bf16[512,4096]{1,0:T(8,128)(2,1)} %reshape.57) | copy-start | bytes 12582916
  134.8 5.7 %copy-start.11 = (bf16[1,384,2048]{2,1,0:T(8,128)(2,1)S(1)}, bf16[1,384,2048]{2,1,0:T(8,128)(2,1)}, u32[]{:S(2)}) copy-start(bf16[1,384,2048]{2,1,0:T(8,128)(2,1)} %param.12) | copy-start | bytes 4718596
  148.6 4.1 %copy-start.6 = (bf16[512,768]{1,0:T(8,128)(2,1)}, bf16[512,768]{1,0:T(8,128)(2,1)S(1)}, u32[]{:S(2)}) copy-start(bf16[512,768]{1,0:T(8,128)(2,1)S(1)} %get-tuple-element.7) | copy-start | bytes 2359300
  148.7 4.1 %copy-start.4 = (bf16[512,768]{1,0:T(8,128)(2,1)}, bf16[512,768]{1,0:T(8,128)(2,1)S(1)}, u32[]{:S(2)}) copy-start(bf16[512,768]{1,0:T(8,128)(2,1)S(1)} %get-tuple-element.5) | copy-start | bytes 2359300
  152.8 3.9 %copy-start.12 = (bf16[1,2048,384]{2,1,0:T(8,128)(2,1)S(1)}, bf16[1,2048,384]{2,1,0:T(8,128)(2,1)}, u32[]{:S(2)}) copy-start(bf16[1,2048,384]{2,1,0:T(8,128)(2,1)} %param.10) | copy-start | bytes 4718596
  170.2 104.5 %all-to-all-start.1 = ((bf16[128,4,4096]{2,1,0:T(4,128)(2,1)}), bf16[128,4,4096]{2,1,0:T(4,128)(2,1)}, u32[]{:S(2)}, u32[]{:S(2)}) async-start(bf16[128,4,4096]{2,1,0:T(4,128)(2,1)} %reshape.58), calls=%async_computation.1 | async-start | bytes 8388608 | tf_op jit(solution)/shard_map/all_to_all | solution.py:70
  182.7 2.2 copy-start.3
  182.7 2.4 copy-start.7
  183.0 10.4 %collective-permute-start.3 = (f32[2048,384]{1,0:T(8,128)S(1)}, f32[2048,384]{1,0:T(8,128)S(1)}, u32[]{:S(2)}, u32[]{:S(2)}) collective-permute-start(f32[2048,384]{1,0:T(8,128)S(1)} %slice_select_fusion.2), channel_id=1, source_target_pairs={{0,1},{1,0},{2,3},{3,2},{4,5},{5,4},{6,7},{7,6},{8,9},{9,8},{10,11... | collective-permute-start | bytes 9437192 | tf_op jit(solution)/shard_map/ppermute | solution.py:77
  186.9 2.0 copy-start.5
  188.9 6.1 %collective-permute-start.4 = (f32[2048,384]{1,0:T(8,128)}, f32[2048,384]{1,0:T(8,128)S(1)}, u32[]{:S(2)}, u32[]{:S(2)}) collective-permute-start(f32[2048,384]{1,0:T(8,128)} %slice_select_fusion.1), channel_id=1, source_target_pairs={{0,1},{1,0},{2,3},{3,2},{4,5},{5,4},{6,7},{7,6},{8,9},{9,8},{10,11... | collective-permute-start | bytes 9437192 | tf_op jit(solution)/shard_map/ppermute | solution.py:77
  192.9 6.4 %collective-permute-start.5 = (f32[384,2048]{1,0:T(8,128)}, f32[384,2048]{1,0:T(8,128)S(1)}, u32[]{:S(2)}, u32[]{:S(2)}) collective-permute-start(f32[384,2048]{1,0:T(8,128)} %slice_select_fusion), channel_id=1, source_target_pairs={{0,1},{1,0},{2,3},{3,2},{4,5},{5,4},{6,7},{7,6},{8,9},{9,8},{10,11... | collective-permute-start | bytes 9437192 | tf_op jit(solution)/shard_map/ppermute | solution.py:77
  201.2 80.4 %copy-start.9 = (bf16[2,128,512]{2,1,0:T(8,128)(2,1)S(1)}, bf16[2,128,512]{2,1,0:T(8,128)(2,1)}, u32[]{:S(2)}) copy-start(bf16[2,128,512]{2,1,0:T(8,128)(2,1)} %copy-done.8) | copy-start | bytes 786436
  274.7 13.1 %copy-start.1 = (bf16[128,2048]{1,0:T(8,128)(2,1)S(1)}, bf16[128,2048]{1,0:T(8,128)(2,1)}, u32[]{:S(2)}) copy-start(bf16[128,2048]{1,0:T(8,128)(2,1)} %param.7) | copy-start | bytes 1572868
